TPU v7x, 256 devices: a whole 4x4x8 slice. The times are simulated.
256 devices in a mesh: grp: 8 (over z), dev: 32 (over y, x, core).
Axes of the slice: x: 4, y: 4, z: 8, core: 2. Of those that a mesh axis runs over, the one named last changes fastest.
Arguments:
- pool: bfloat16 [786432, 1024], P(('grp', 'dev'))
- nearest: float32 [786432], P(('grp', 'dev')), may hold values from 0.5 to 2.2
- center_owner: int32 [8, 256], P('grp'), may hold values from 0 to 31, as said below
- center_offset: int32 [8, 256], P('grp'), may hold values from 0 to 3071
Outputs:
- nearest_after: float32 [786432], P(('grp', 'dev'))
Inputs may be any that keep to these rules, and one draw needn't show every extreme that they name: `center_owner`: in each group no more than 32 centers have the same owner, one owner has exactly 32, and the centers of a group are distinct rows.
All inputs are finite; a program needn't handle non-finite values.
Results may differ from a plain program's by a relative error of at most 0.0003.
Values may be sent and summed in bfloat16 or wider, within the bound.
No kernel may reach another device: no remote copies, remote signals or barrier semaphores. Data moves between devices by JAX's collectives and lax.ppermute only.
A program may use at most 64 MiB of HBM per device.

v0:
```python
import math
import jax
import jax.numpy as jnp
from jax import lax
from jax.sharding import PartitionSpec as P

MOST = 32


def nearest_fold(pool_rows, row_norm, running, fragment):
    center_norm = jnp.einsum("cd,cd->c", fragment, fragment, preferred_element_type=jnp.float32)
    total_rows = pool_rows.shape[0]
    block = math.gcd(total_rows, 512)
    blocks = total_rows // block

    def one_block(args):
        block_rows, block_norm, block_near = args
        inner = lax.dot_general(
            block_rows, fragment, (((1,), (1,)), ((), ())), preferred_element_type=jnp.float32
        )
        distance = jnp.maximum(block_norm[:, None] + center_norm[None, :] - 2.0 * inner, 0.0)
        return jnp.minimum(block_near, jnp.min(distance, axis=1))

    result = lax.map(
        one_block,
        (
            pool_rows.reshape(blocks, block, pool_rows.shape[1]),
            row_norm.reshape(blocks, block),
            running.reshape(blocks, block),
        ),
    )
    return result.reshape(total_rows)


def shards(pool, nearest, center_owner, center_offset):
    owners = center_owner[0]
    offsets = center_offset[0]
    dev_count = lax.axis_size("dev")
    my_index = lax.axis_index("dev")
    per_device = owners.shape[0] // dev_count
    owner_hot = (owners[:, None] == jnp.arange(dev_count, dtype=jnp.int32)[None, :]).astype(
        jnp.int32
    )
    slot_rank = jnp.sum((jnp.cumsum(owner_hot, axis=0) - 1) * owner_hot, axis=1)
    chosen = (
        (owners == my_index)[None, :]
        & (slot_rank[None, :] == jnp.arange(MOST, dtype=jnp.int32)[:, None])
    ).astype(jnp.int32)
    slot_offsets = jnp.sum(chosen * offsets[None, :], axis=1)
    slot_rows = jnp.take(pool, slot_offsets, axis=0)
    every_slot = lax.all_gather(slot_rows, "dev", axis=0, tiled=True)
    slot_index = owners * MOST + slot_rank
    mine = lax.dynamic_slice_in_dim(slot_index, my_index * per_device, per_device)
    local_centers = jnp.take(every_slot, mine, axis=0)
    row_norm = jnp.einsum("rd,rd->r", pool, pool, preferred_element_type=jnp.float32)
    return nearest_fold(
        pool, row_norm, nearest, lax.all_gather(local_centers, ("grp", "dev"), axis=0, tiled=True)
    )


def solution(mesh):
    in_specs = (P(("grp", "dev"), None), P(("grp", "dev")), P("grp", None), P("grp", None))
    out_specs = P(("grp", "dev"))
    return jax.shard_map(shards, mesh=mesh, in_specs=in_specs, out_specs=out_specs, check_vma=False)
```

profile of v0, /device:TPU:1, one launch (start us, length us, event | category | flops | bytes accessed | tf_op | source)
XLA Modules:
  0.0 228.6 jit_solution(5956748127939711534)
XLA Ops:
  6.5 0.0 copy-start
  6.5 0.0 all-gather.3.cloned.1.call-start
  6.5 0.7 fusion.7
  7.2 0.6 reduce-window.6
  7.8 0.2 slice_reduce_fusion
  8.0 0.7 compare_reduce_fusion
  8.7 0.8 fusion.6
  9.5 0.8 select_reduce_fusion
  10.3 4.3 %gather_fusion = bf16[32,1024]{1,0:T(8,128)(2,1)S(1)} fusion(bf16[3072,1024]{1,0:T(8,128)(2,1)} %param.6, s32[1024]{0:T(1024)S(1)} %pad_clamp_fusion.1), kind=kCustom, calls=%fused_computation | custom fusion | bytes 131200 | tf_op jit(solution)/shard_map/jit(_take)/gather | solution.py:50
  14.6 0.7 broadcast_select_fusion
  15.3 0.0 all-gather.3.cloned.1.call-update
  15.3 0.0 all-gather.5.cloned.1.call-start
  15.4 0.7 multiply_add_fusion
  16.1 0.1 compare_and_fusion.1
  16.2 52.4 %all-gather.3.cloned.1.call-done = bf16[1024,1024]{1,0:T(8,128)(2,1)} async-done(((bf16[32,1024]{1,0:T(8,128)(2,1)}), bf16[1024,1024]{1,0:T(8,128)(2,1)}) %all-gather.3.cloned.1.call-update) | async-done | bytes 2097168 | tf_op jit(solution)/shard_map/all_gather | solution.py:51
  68.6 2.4 %gather_fusion.1 = bf16[8,1024]{1,0:T(8,128)(2,1)S(1)} fusion(bf16[1024,1024]{1,0:T(8,128)(2,1)} %all-gather.3.cloned.1.call-done, s32[1024]{0:T(1024)S(1)} %pad_clamp_fusion), kind=kCustom, calls=%fused_computation.1 | custom fusion | bytes 32800 | tf_op jit(solution)/shard_map/jit(_take)/gather | solution.py:54
  71.0 0.7 broadcast_select_fusion.1
  71.7 0.0 all-gather.5.cloned.1.call-update
  71.7 4.1 %fusion.3 = f32[3072]{0:T(1024)S(1)} fusion(bf16[3072,1024]{1,0:T(8,128)(2,1)} %param.6), kind=kLoop, calls=%fused_computation.9 | loop fusion | flops 9434112 | bytes 6303744 | tf_op jit(solution)/shard_map/rd,rd->r/dot_general | solution.py:55
  75.8 0.0 copy-done
  75.9 110.8 %all-gather.5.cloned.1.call-done = bf16[2048,1024]{1,0:T(8,128)(2,1)} async-done(((bf16[8,1024]{1,0:T(8,128)(2,1)}), bf16[2048,1024]{1,0:T(8,128)(2,1)}) %all-gather.5.cloned.1.call-update) | async-done | bytes 4194320 | tf_op jit(solution)/shard_map/all_gather | solution.py:57
  186.6 3.1 %fusion.4 = f32[2048]{0:T(1024)S(1)} fusion(bf16[2048,1024]{1,0:T(8,128)(2,1)} %all-gather.5.cloned.1.call-done), kind=kLoop, calls=%fused_computation.11 | loop fusion | flops 6289408 | bytes 4202496 | tf_op jit(solution)/shard_map/cd,cd->c/dot_general | solution.py:11
  189.7 31.4 %while.10 = (s32[]{:T(128)}, f32[6,512]{1,0:T(8,128)S(1)}, f32[6,512]{1,0:T(8,128)S(1)}, f32[6,512]{1,0:T(8,128)S(1)}, f32[2048]{0:T(1024)S(1)}, /*index=5*/bf16...) while((s32[]{:T(128)}, f32[6,512]{1,0:T(8,128)S(1)}, f32[6,512]{1,0:T(8,128)S(1)}, ...), condition=%wide.region_6.7_spmd, body=%wide.region_4.6_spmd.sunk | while | flops 2152726528 | bytes 5270121 | solution.py:24
  189.7 5.1 %maximum_reduce_fusion.2 = f32[512]{0:T(512)S(1)} fusion(bf16[2048,1024]{1,0:T(8,128)(2,1)} %get-tuple-element.126, f32[2048]{0:T(1024)S(1)} %get-tuple-element.124, f32[512]{0:T(512)S(1)} %bitcast.39, bf16[6,512,1024]{2,1,0:T(8,128)(2,1)} %get-tuple-element.125, s32[]{:T(128)} %get-tuple-element.111), kind=kOutput, calls=%fused_computation.2.clone.1 | convolution fusion | flops 2152726016 | bytes 5255680 | tf_op jit(solution)/shard_map/while/body/eval_jaxpr/dot_general | solution.py:18
  194.9 0.1 dynamic_update_slice.5
  195.0 5.1 %maximum_reduce_fusion.2 = f32[512]{0:T(512)S(1)} fusion(bf16[2048,1024]{1,0:T(8,128)(2,1)} %get-tuple-element.126, f32[2048]{0:T(1024)S(1)} %get-tuple-element.124, f32[512]{0:T(512)S(1)} %bitcast.39, bf16[6,512,1024]{2,1,0:T(8,128)(2,1)} %get-tuple-element.125, s32[]{:T(128)} %get-tuple-element.111), kind=kOutput, calls=%fused_computation.2.clone.1 | convolution fusion | flops 2152726016 | bytes 5255680 | tf_op jit(solution)/shard_map/while/body/eval_jaxpr/dot_general | solution.py:18
  200.1 0.1 dynamic_update_slice.5
  200.2 5.1 %maximum_reduce_fusion.2 = f32[512]{0:T(512)S(1)} fusion(bf16[2048,1024]{1,0:T(8,128)(2,1)} %get-tuple-element.126, f32[2048]{0:T(1024)S(1)} %get-tuple-element.124, f32[512]{0:T(512)S(1)} %bitcast.39, bf16[6,512,1024]{2,1,0:T(8,128)(2,1)} %get-tuple-element.125, s32[]{:T(128)} %get-tuple-element.111), kind=kOutput, calls=%fused_computation.2.clone.1 | convolution fusion | flops 2152726016 | bytes 5255680 | tf_op jit(solution)/shard_map/while/body/eval_jaxpr/dot_general | solution.py:18
  205.3 0.1 dynamic_update_slice.5
  205.4 5.1 %maximum_reduce_fusion.2 = f32[512]{0:T(512)S(1)} fusion(bf16[2048,1024]{1,0:T(8,128)(2,1)} %get-tuple-element.126, f32[2048]{0:T(1024)S(1)} %get-tuple-element.124, f32[512]{0:T(512)S(1)} %bitcast.39, bf16[6,512,1024]{2,1,0:T(8,128)(2,1)} %get-tuple-element.125, s32[]{:T(128)} %get-tuple-element.111), kind=kOutput, calls=%fused_computation.2.clone.1 | convolution fusion | flops 2152726016 | bytes 5255680 | tf_op jit(solution)/shard_map/while/body/eval_jaxpr/dot_general | solution.py:18
  210.6 0.1 dynamic_update_slice.5
  210.7 5.1 %maximum_reduce_fusion.2 = f32[512]{0:T(512)S(1)} fusion(bf16[2048,1024]{1,0:T(8,128)(2,1)} %get-tuple-element.126, f32[2048]{0:T(1024)S(1)} %get-tuple-element.124, f32[512]{0:T(512)S(1)} %bitcast.39, bf16[6,512,1024]{2,1,0:T(8,128)(2,1)} %get-tuple-element.125, s32[]{:T(128)} %get-tuple-element.111), kind=kOutput, calls=%fused_computation.2.clone.1 | convolution fusion | flops 2152726016 | bytes 5255680 | tf_op jit(solution)/shard_map/while/body/eval_jaxpr/dot_general | solution.py:18
  215.8 0.1 dynamic_update_slice.5
  215.9 5.1 %maximum_reduce_fusion.2 = f32[512]{0:T(512)S(1)} fusion(bf16[2048,1024]{1,0:T(8,128)(2,1)} %get-tuple-element.126, f32[2048]{0:T(1024)S(1)} %get-tuple-element.124, f32[512]{0:T(512)S(1)} %bitcast.39, bf16[6,512,1024]{2,1,0:T(8,128)(2,1)} %get-tuple-element.125, s32[]{:T(128)} %get-tuple-element.111), kind=kOutput, calls=%fused_computation.2.clone.1 | convolution fusion | flops 2152726016 | bytes 5255680 | tf_op jit(solution)/shard_map/while/body/eval_jaxpr/dot_general | solution.py:18
  221.0 0.1 dynamic_update_slice.5
  221.1 0.6 reshape.63
  (21 shorter events, 0.2 us)
Async XLA Ops:
  6.5 69.3 %copy-start = (f32[3072]{0:T(1024)S(1)}, f32[3072]{0:T(1024)}, u32[]{:S(2)}) copy-start(f32[3072]{0:T(1024)} %param.7) | copy-start | bytes 36868
  6.5 62.0 %all-gather.3.cloned.1.call-start = ((), (), s32[]{:S(2)}) async-start(), calls=%async_computation | async-start | bytes 2162688 | tf_op jit(solution)/shard_map/all_gather | solution.py:51
  15.3 171.3 %all-gather.5.cloned.1.call-start = ((), (), s32[]{:S(2)}) async-start(), calls=%async_computation.1 | async-start | bytes 4210688 | tf_op jit(solution)/shard_map/all_gather | solution.py:57
Sparse Core Ops, SparseCore 0:
  15.5 53.0 all-gather.2
  72.2 114.3 all-gather.4
where the time goes:
time: 229 us
  waiting for transfers between devices  163 us (71%)
  matrix products  30.7 us (13%)
  between operations  13.5 us (6%)
  other arithmetic  13 us (6%)
  local copies, waits for them, and re-layouts  7.93 us (3%)
    all_gather x1, waiting for transfers between devices, shards(): lax.all_gather(local_centers, ('grp', 'dev'), axis=0, tiled=True)  111 us
    all_gather x1, waiting for transfers between devices, shards(): every_slot = lax.all_gather(slot_rows, 'dev', axis=0, tiled=True)  52.4 us
    dot_general x6, matrix products, one_block(): lax.dot_general(block_rows, fragment, (((1,), (1,)), ((), ())), preferred...  30.7 us
  transfers between devices with their start and end apart: 2, of which 2 were waited for; matrix products, arithmetic and copies ran while one was open for 2% of the time, Pallas kernels for 0%

commit v1 on v0

--- a/solution.py
+++ b/solution.py
@@ -5,6 +5,13 @@
 from jax.sharding import PartitionSpec as P
 
 MOST = 32
+
+
+def all_by_exchange(x, axis, dim):
+    size = lax.axis_size(axis)
+    blocks = jnp.stack([x for _ in range(size)])
+    blocks = lax.all_to_all(blocks, axis, split_axis=0, concat_axis=0)
+    return jnp.concatenate(blocks, axis=dim)
 
 
 def nearest_fold(pool_rows, row_norm, running, fragment):
@@ -48,7 +55,7 @@
     ).astype(jnp.int32)
     slot_offsets = jnp.sum(chosen * offsets[None, :], axis=1)
     slot_rows = jnp.take(pool, slot_offsets, axis=0)
-    every_slot = lax.all_gather(slot_rows, "dev", axis=0, tiled=True)
+    every_slot = all_by_exchange(slot_rows, "dev", 0)
     slot_index = owners * MOST + slot_rank
     mine = lax.dynamic_slice_in_dim(slot_index, my_index * per_device, per_device)
     local_centers = jnp.take(every_slot, mine, axis=0)

time: 229 us -> 213 us (0.930)
  waiting for transfers between devices: 163 us -> 140 us
  starting transfers between devices: 0.04 us -> 8.63 us
    all_gather x1 -> x0, waiting for transfers between devices: 52.4 us -> none  [shards(): every_slot = lax.all_gather(slot_rows, 'dev', axis=0, tiled=True)]
    all_to_all x0 -> x1, waiting for transfers between devices: none -> 27.7 us  [all_by_exchange(): blocks = lax.all_to_all(blocks, axis, split_axis=0, concat_axis=0)]
    all_to_all x0 -> x1, starting transfers between devices: none -> 8.59 us  [all_by_exchange(): blocks = lax.all_to_all(blocks, axis, split_axis=0, concat_axis=0)]
where the time goes in v1:
time: 213 us; the launch traced here: 212 us
  waiting for transfers between devices  140 us (66%)
  matrix products  30.7 us (14%)
  between operations  13.5 us (6%)
  other arithmetic  11.7 us (5%)
  starting transfers between devices  8.63 us (4%)
  local copies, waits for them, and re-layouts  7.68 us (4%)
    all_gather x1, waiting for transfers between devices, shards(): lax.all_gather(local_centers, ('grp', 'dev'), axis=0, tiled=True)  112 us
    dot_general x6, matrix products, one_block(): lax.dot_general(block_rows, fragment, (((1,), (1,)), ((), ())), preferred...  30.7 us
    all_to_all x1, waiting for transfers between devices, all_by_exchange(): blocks = lax.all_to_all(blocks, axis, split_axis=0, concat_axis=0)  27.7 us
    all_to_all x1, starting transfers between devices, all_by_exchange(): blocks = lax.all_to_all(blocks, axis, split_axis=0, concat_axis=0)  8.59 us
    gather x1, local copies, waits for them, and re-layouts, shards(): slot_rows = jnp.take(pool, slot_offsets, axis=0)  4.27 us
  transfers between devices with their start and end apart: 2, of which 2 were waited for; matrix products, arithmetic and copies ran while one was open for 2% of the time, Pallas kernels for 0%

profile of v1, /device:TPU:1, one launch (start us, length us, event | category | flops | bytes accessed | tf_op | source)
XLA Modules:
  0.0 212.2 jit_solution(14937177414396744674)
XLA Ops:
  6.5 0.0 copy-start
  6.5 0.8 fusion.7
  7.3 0.6 reduce-window.6
  7.9 0.2 slice_reduce_fusion
  8.1 0.7 compare_reduce_fusion
  8.8 0.8 fusion.6
  9.6 0.8 select_reduce_fusion
  10.4 4.3 %gather_fusion = bf16[32,1024]{1,0:T(8,128)(2,1)S(1)} fusion(bf16[3072,1024]{1,0:T(8,128)(2,1)} %param.6, s32[1024]{0:T(1024)S(1)} %pad_clamp_fusion.1), kind=kCustom, calls=%fused_computation | custom fusion | bytes 131200 | tf_op jit(solution)/shard_map/jit(_take)/gather | solution.py:57
  14.7 0.1 broadcast_select_fusion
  14.8 1.6 stack.2
  16.4 8.6 %all-to-all-start = ((bf16[32,32,1024]{2,1,0:T(8,128)(2,1)}), bf16[32,32,1024]{2,1,0:T(8,128)(2,1)S(1)}, u32[]{:S(2)}, u32[]{:S(2)}) async-start(bf16[32,32,1024]{2,1,0:T(8,128)(2,1)} %stack.2), calls=%async_computation | async-start | bytes 4194304 | tf_op jit(solution)/shard_map/all_to_all | solution.py:13
  25.0 0.0 copy-start.1
  25.0 0.0 all-gather.2.cloned.1.call-start
  25.0 0.0 copy-done
  25.1 0.1 compare_and_fusion.1
  25.1 27.7 %all-to-all-done = bf16[32,32,1024]{2,1,0:T(8,128)(2,1)S(1)} async-done(((bf16[32,32,1024]{2,1,0:T(8,128)(2,1)}), bf16[32,32,1024]{2,1,0:T(8,128)(2,1)S(1)}, u32[]{:S(2)}, u32[]{:S(2)}) %all-to-all-start) | async-done | bytes 2097184 | tf_op jit(solution)/shard_map/all_to_all | solution.py:13
  52.8 0.6 gather_fusion.1
  53.4 0.7 broadcast_select_fusion.1
  54.1 0.0 all-gather.2.cloned.1.call-update
  54.1 4.1 %fusion.3 = f32[3072]{0:T(1024)S(1)} fusion(bf16[3072,1024]{1,0:T(8,128)(2,1)} %param.6), kind=kLoop, calls=%fused_computation.9 | loop fusion | flops 9434112 | bytes 6303744 | tf_op jit(solution)/shard_map/rd,rd->r/dot_general | solution.py:62
  58.2 0.0 copy-done.1
  58.2 112.0 %all-gather.2.cloned.1.call-done = bf16[2048,1024]{1,0:T(8,128)(2,1)} async-done(((bf16[8,1024]{1,0:T(8,128)(2,1)}), bf16[2048,1024]{1,0:T(8,128)(2,1)}) %all-gather.2.cloned.1.call-update) | async-done | bytes 4194320 | tf_op jit(solution)/shard_map/all_gather | solution.py:64
  170.2 3.1 %fusion.4 = f32[2048]{0:T(1024)S(1)} fusion(bf16[2048,1024]{1,0:T(8,128)(2,1)} %all-gather.2.cloned.1.call-done), kind=kLoop, calls=%fused_computation.11 | loop fusion | flops 6289408 | bytes 4202496 | tf_op jit(solution)/shard_map/cd,cd->c/dot_general | solution.py:18
  173.3 31.4 %while.10 = (s32[]{:T(128)}, f32[6,512]{1,0:T(8,128)S(1)}, f32[6,512]{1,0:T(8,128)S(1)}, f32[6,512]{1,0:T(8,128)S(1)}, f32[2048]{0:T(1024)S(1)}, /*index=5*/bf16...) while((s32[]{:T(128)}, f32[6,512]{1,0:T(8,128)S(1)}, f32[6,512]{1,0:T(8,128)S(1)}, ...), condition=%wide.region_6.7_spmd, body=%wide.region_4.6_spmd.sunk | while | flops 2152726528 | bytes 5270121 | solution.py:31
  173.3 5.1 %maximum_reduce_fusion.2 = f32[512]{0:T(512)S(1)} fusion(bf16[2048,1024]{1,0:T(8,128)(2,1)} %get-tuple-element.126, f32[2048]{0:T(1024)S(1)} %get-tuple-element.124, f32[512]{0:T(512)S(1)} %bitcast.41, bf16[6,512,1024]{2,1,0:T(8,128)(2,1)} %get-tuple-element.125, s32[]{:T(128)} %get-tuple-element.111), kind=kOutput, calls=%fused_computation.2.clone.1 | convolution fusion | flops 2152726016 | bytes 5255680 | tf_op jit(solution)/shard_map/while/body/eval_jaxpr/dot_general | solution.py:25
  178.5 0.1 dynamic_update_slice.5
  178.6 5.1 %maximum_reduce_fusion.2 = f32[512]{0:T(512)S(1)} fusion(bf16[2048,1024]{1,0:T(8,128)(2,1)} %get-tuple-element.126, f32[2048]{0:T(1024)S(1)} %get-tuple-element.124, f32[512]{0:T(512)S(1)} %bitcast.41, bf16[6,512,1024]{2,1,0:T(8,128)(2,1)} %get-tuple-element.125, s32[]{:T(128)} %get-tuple-element.111), kind=kOutput, calls=%fused_computation.2.clone.1 | convolution fusion | flops 2152726016 | bytes 5255680 | tf_op jit(solution)/shard_map/while/body/eval_jaxpr/dot_general | solution.py:25
  183.7 0.1 dynamic_update_slice.5
  183.8 5.1 %maximum_reduce_fusion.2 = f32[512]{0:T(512)S(1)} fusion(bf16[2048,1024]{1,0:T(8,128)(2,1)} %get-tuple-element.126, f32[2048]{0:T(1024)S(1)} %get-tuple-element.124, f32[512]{0:T(512)S(1)} %bitcast.41, bf16[6,512,1024]{2,1,0:T(8,128)(2,1)} %get-tuple-element.125, s32[]{:T(128)} %get-tuple-element.111), kind=kOutput, calls=%fused_computation.2.clone.1 | convolution fusion | flops 2152726016 | bytes 5255680 | tf_op jit(solution)/shard_map/while/body/eval_jaxpr/dot_general | solution.py:25
  188.9 0.1 dynamic_update_slice.5
  189.0 5.1 %maximum_reduce_fusion.2 = f32[512]{0:T(512)S(1)} fusion(bf16[2048,1024]{1,0:T(8,128)(2,1)} %get-tuple-element.126, f32[2048]{0:T(1024)S(1)} %get-tuple-element.124, f32[512]{0:T(512)S(1)} %bitcast.41, bf16[6,512,1024]{2,1,0:T(8,128)(2,1)} %get-tuple-element.125, s32[]{:T(128)} %get-tuple-element.111), kind=kOutput, calls=%fused_computation.2.clone.1 | convolution fusion | flops 2152726016 | bytes 5255680 | tf_op jit(solution)/shard_map/while/body/eval_jaxpr/dot_general | solution.py:25
  194.2 0.1 dynamic_update_slice.5
  194.3 5.1 %maximum_reduce_fusion.2 = f32[512]{0:T(512)S(1)} fusion(bf16[2048,1024]{1,0:T(8,128)(2,1)} %get-tuple-element.126, f32[2048]{0:T(1024)S(1)} %get-tuple-element.124, f32[512]{0:T(512)S(1)} %bitcast.41, bf16[6,512,1024]{2,1,0:T(8,128)(2,1)} %get-tuple-element.125, s32[]{:T(128)} %get-tuple-element.111), kind=kOutput, calls=%fused_computation.2.clone.1 | convolution fusion | flops 2152726016 | bytes 5255680 | tf_op jit(solution)/shard_map/while/body/eval_jaxpr/dot_general | solution.py:25
  199.4 0.1 dynamic_update_slice.5
  199.5 5.1 %maximum_reduce_fusion.2 = f32[512]{0:T(512)S(1)} fusion(bf16[2048,1024]{1,0:T(8,128)(2,1)} %get-tuple-element.126, f32[2048]{0:T(1024)S(1)} %get-tuple-element.124, f32[512]{0:T(512)S(1)} %bitcast.41, bf16[6,512,1024]{2,1,0:T(8,128)(2,1)} %get-tuple-element.125, s32[]{:T(128)} %get-tuple-element.111), kind=kOutput, calls=%fused_computation.2.clone.1 | convolution fusion | flops 2152726016 | bytes 5255680 | tf_op jit(solution)/shard_map/while/body/eval_jaxpr/dot_general | solution.py:25
  204.7 0.1 dynamic_update_slice.5
  204.7 0.6 reshape.74
  (22 shorter events, 0.2 us)
Async XLA Ops:
  6.5 18.5 %copy-start = (s32[1,256]{1,0:T(1,128)S(1)}, s32[1,256]{1,0:T(1,128)}, u32[]{:S(2)}) copy-start(s32[1,256]{1,0:T(1,128)} %param.8) | copy-start | bytes 3076
  16.4 36.4 %all-to-all-start = ((bf16[32,32,1024]{2,1,0:T(8,128)(2,1)}), bf16[32,32,1024]{2,1,0:T(8,128)(2,1)S(1)}, u32[]{:S(2)}, u32[]{:S(2)}) async-start(bf16[32,32,1024]{2,1,0:T(8,128)(2,1)} %stack.2), calls=%async_computation | async-start | bytes 4194304 | tf_op jit(solution)/shard_map/all_to_all | solution.py:13
  25.0 33.2 %copy-start.1 = (f32[3072]{0:T(1024)S(1)}, f32[3072]{0:T(1024)}, u32[]{:S(2)}) copy-start(f32[3072]{0:T(1024)} %param.7) | copy-start | bytes 36868
  25.0 145.2 %all-gather.2.cloned.1.call-start = ((), (), s32[]{:S(2)}) async-start(), calls=%async_computation.1 | async-start | bytes 4210688 | tf_op jit(solution)/shard_map/all_gather | solution.py:64
Sparse Core Ops, SparseCore 0:
  54.2 115.9 all-gather.1
